TPU v7x, 512 devices: a whole 4x8x8 slice. The times are simulated.
512 devices in a mesh: section: 8 (over z), ctx: 8 (over y_hi, x), tp: 8 (over y_lo, core).
Axes of the slice: x: 4, y: 8 (y_hi: 2, y_lo: 4; y = y_hi * 4 + y_lo), z: 8, core: 2. Of those that a mesh axis runs over, the one named last changes fastest.
Arguments:
- block_order: int32 [16], replicated, may hold values from 0 to 15, each once
- plan: int32 [8], replicated, may hold values from 0 to 1
- q_box: bfloat16 [8, 2, 1408, 8192], P('section', None, 'ctx', 'tp'), may hold values from -8 to 8
- k_box: bfloat16 [8, 2, 1408, 1024], P('section', None, ('ctx', 'tp')), may hold values from -8 to 8
- v_box: bfloat16 [8, 2, 1408, 1024], P('section', None, ('ctx', 'tp')), may hold values from -6 to 6
- grad_out: bfloat16 [8, 1408, 8192], P('section', 'ctx', 'tp'), may hold values from -6 to 6
Outputs:
- attn_out: bfloat16 [8, 1408, 8192], P('section', 'ctx', 'tp')
- grad_q: bfloat16 [8, 1408, 8192], P('section', 'ctx', 'tp')
- grad_k: float32 [8, 1408, 1024], P('section', ('ctx', 'tp'))
- grad_v: float32 [8, 1408, 1024], P('section', ('ctx', 'tp'))
Inputs may be any that keep to these rules, and one draw needn't show every extreme that they name: `block_order`: a permutation: every block sits in exactly one storage slot, slot j covering storage rows j * 88 to (j + 1) * 88 - 1.
All inputs are finite; a program needn't handle non-finite values.
Results may differ from a plain program's by a relative error of at most 0.012.
Values may be sent and summed in bfloat16 or wider, within the bound.
No kernel may reach another device: no remote copies, remote signals or barrier semaphores. Data moves between devices by JAX's collectives and lax.ppermute only.
A program may use at most 64 MiB of HBM per device.

v0:
```python
import jax
import jax.numpy as jnp
from jax import lax
from jax.sharding import PartitionSpec as P

HEAD_DIM = 128
NEG = -1e30


def passed_along(block, axis, distance):
    devices = range(lax.axis_size(axis))
    route = [((i - distance) % len(devices), i) for i in devices]
    return lax.ppermute(block, axis, route)


def body(block_order, plan, q_box, k_box, v_box, grad_out):
    tp_count = lax.axis_size("tp")
    ctx_count = lax.axis_size("ctx")
    section_count = lax.axis_size("section")
    tok_rows = q_box.shape[2]
    kv_rows = k_box.shape[2]
    seq_rows = tok_rows * ctx_count
    block_len = seq_rows // block_order.shape[0]
    head_size = HEAD_DIM
    heads_local = q_box.shape[3] // head_size
    kv_local = k_box.shape[3] // head_size // tp_count
    group = heads_local // kv_local
    kv_width = kv_local * head_size
    scale = head_size ** (-0.5)
    section_rank = lax.axis_index("section")
    receiver = (section_rank + 1) % section_count
    wanted = lax.dynamic_index_in_dim(plan, receiver, 0, keepdims=False)
    q_send = lax.dynamic_index_in_dim(q_box[0], wanted, 0, keepdims=False)
    k_send = lax.dynamic_index_in_dim(k_box[0], wanted, 0, keepdims=False)
    v_send = lax.dynamic_index_in_dim(v_box[0], wanted, 0, keepdims=False)
    kv_send = jnp.stack(
        [k_send.reshape(kv_rows, -1, head_size), v_send.reshape(kv_rows, -1, head_size)], axis=2
    ).reshape(kv_rows, -1)
    queries, kv_rows_in = passed_along((q_send, kv_send), "section", 1)
    cotangent = passed_along(grad_out[0], "section", -1)
    kv_tok = lax.all_to_all(kv_rows_in, "tp", split_axis=1, concat_axis=0, tiled=True)
    kv_full = lax.all_gather(kv_tok, "ctx", axis=0, tiled=True)
    kv_full = kv_full.reshape(seq_rows, kv_local, 2, head_size)
    key_heads = kv_full[:, :, 0, :]
    value_heads = kv_full[:, :, 1, :]
    positions = (
        block_order[:, None] * block_len + jnp.arange(block_len, dtype=jnp.int32)[None, :]
    ).reshape(seq_rows)
    query_pos = lax.dynamic_slice_in_dim(positions, lax.axis_index("ctx") * tok_rows, tok_rows)
    visible = (positions[None, :] <= query_pos[:, None])[None, None]
    q4 = queries.reshape(tok_rows, kv_local, group, head_size)
    do4 = cotangent.reshape(tok_rows, kv_local, group, head_size)
    scores = jnp.einsum("qgjd,kgd->gjqk", q4, key_heads, preferred_element_type=jnp.float32) * scale
    scores = jnp.where(visible, scores, NEG)
    top_score = jnp.max(scores, axis=-1, keepdims=True)
    totals = jnp.sum(jnp.where(visible, jnp.exp(scores - top_score), 0.0), axis=-1, keepdims=True)
    log_total = top_score + jnp.log(totals)
    probs = jnp.where(visible, jnp.exp(scores - log_total), 0.0)
    probs_low = probs.astype(jnp.bfloat16)
    attended = jnp.einsum(
        "gjqk,kgd->qgjd", probs_low, value_heads, preferred_element_type=jnp.float32
    )
    delta = jnp.sum(do4.astype(jnp.float32) * attended, axis=-1)
    dprobs = jnp.einsum("qgjd,kgd->gjqk", do4, value_heads, preferred_element_type=jnp.float32)
    dscores = (probs * (dprobs - jnp.transpose(delta, (1, 2, 0))[..., None])).astype(jnp.bfloat16)
    q_grad = (
        jnp.einsum("gjqk,kgd->qgjd", dscores, key_heads, preferred_element_type=jnp.float32) * scale
    ).astype(jnp.bfloat16)
    key_grad = jnp.einsum("gjqk,qgjd->kgd", dscores, q4, preferred_element_type=jnp.float32) * scale
    value_grad = jnp.einsum("gjqk,qgjd->kgd", probs_low, do4, preferred_element_type=jnp.float32)
    attended_flat = attended.astype(jnp.bfloat16).reshape(tok_rows, heads_local * head_size)
    q_grad_flat = q_grad.reshape(tok_rows, heads_local * head_size)
    grad_terms = jnp.stack([key_grad, value_grad], axis=2).reshape(seq_rows, 2 * kv_width)
    own_grads = lax.psum_scatter(grad_terms, "ctx", scatter_dimension=0, tiled=True)
    tok_grads = lax.all_to_all(own_grads, "tp", split_axis=0, concat_axis=1, tiled=True)
    tok_grads = tok_grads.reshape(kv_rows, -1, 2, head_size)
    k_grad_tokens = tok_grads[:, :, 0, :].reshape(kv_rows, -1)
    v_grad_tokens = tok_grads[:, :, 1, :].reshape(kv_rows, -1)
    return (attended_flat[None], q_grad_flat[None], k_grad_tokens[None], v_grad_tokens[None])


def solution(mesh):
    in_specs = (
        P(),
        P(),
        P("section", None, "ctx", "tp"),
        P("section", None, ("ctx", "tp"), None),
        P("section", None, ("ctx", "tp"), None),
        P("section", "ctx", "tp"),
    )
    out_specs = (
        P("section", "ctx", "tp"),
        P("section", "ctx", "tp"),
        P("section", ("ctx", "tp"), None),
        P("section", ("ctx", "tp"), None),
    )
    return jax.shard_map(body, mesh=mesh, in_specs=in_specs, out_specs=out_specs, check_vma=False)
```

profile of v0, /device:TPU:1, one launch (start us, length us, event | category | flops | bytes accessed | tf_op | source)
XLA Modules:
  0.0 212.7 jit_solution(3541561579943129193)
XLA Ops:
  7.2 0.0 copy-start
  7.2 11.6 %collective-permute-start.2 = (bf16[176,1024]{1,0:T(8,128)(2,1)}, bf16[176,1024]{1,0:T(8,128)(2,1)S(1)}, u32[]{:S(2)}, u32[]{:S(2)}) collective-permute-start(bf16[176,1024]{1,0:T(8,128)(2,1)} %bitcast.163), channel_id=1, source_target_pairs={{64,0},{128,64},{192,128},{256,192},{320,256},{384,320},{448,384},... | collective-permute-start | bytes 1081352 | tf_op jit(solution)/shard_map/ppermute | solution.py:13
  18.8 1.2 dynamic_slice.18
  22.0 1.5 dynamic-slice_reduce_fusion
  23.6 0.1 copy.26
  23.7 1.9 collective-permute-start
  25.6 0.0 copy-done
  25.6 0.8 dynamic-slice_bitcast_fusion
  26.4 1.9 collective-permute-start.1
  28.3 0.7 broadcast_multiply_fusion
  29.0 0.1 iota_add_fusion
  29.1 0.1 add.59
  29.1 0.1 dynamic_slice.21
  29.2 1.0 collective-permute-done
  30.3 0.7 copy.27
  31.0 7.0 %all-to-all-start = ((bf16[22,8,256]{2,0,1:T(8,128)(2,1)}), bf16[22,8,256]{2,0,1:T(8,128)(2,1)S(1)}, u32[]{:S(2)}, u32[]{:S(2)}) async-start(bf16[22,8,256]{2,0,1:T(8,128)(2,1)} %copy.27), calls=%async_computation | async-start | bytes 196608 | tf_op jit(solution)/shard_map/all_to_all | solution.py:41
  37.9 0.0 reduce-scatter.2.cloned.1.call-start
  37.9 0.2 broadcast_compare_fusion
  38.2 5.1 %all-to-all-done = bf16[22,8,256]{2,0,1:T(8,128)(2,1)S(1)} async-done(((bf16[22,8,256]{2,0,1:T(8,128)(2,1)}), bf16[22,8,256]{2,0,1:T(8,128)(2,1)S(1)}, u32[]{:S(2)}, u32[]{:S(2)}) %all-to-all-start) | async-done | bytes 90144 | tf_op jit(solution)/shard_map/all_to_all | solution.py:41
  43.3 41.5 %all_gather.3 = bf16[1408,256]{1,0:T(8,128)(2,1)S(1)} all-gather(bf16[176,256]{1,0:T(8,128)(2,1)S(1)} %all_to_all.29), channel_id=1, replica_groups=mesh['section'=8,'ctx'=8,'tp'=8] {'ctx'}, dimensions={0}, use_global_device_ids=true | all-gather | bytes 811008 | tf_op jit(solution)/shard_map/all_gather | solution.py:42
  84.9 0.3 copy.28
  85.2 0.0 collective-permute-done.2
  85.2 0.1 convert_bitcast_fusion
  85.3 0.1 copy.47
  85.4 0.0 collective-permute-done.1
  85.4 2.0 fusion.30
  87.4 2.0 select_reduce_fusion
  89.4 0.1 copy.48
  89.5 1.8 fusion.18
  91.3 2.7 %fusion.6 = bf16[8,176,1408]{2,1,0:T(8,128)(2,1)S(1)} fusion(f32[8,176]{1,0:T(8,128)S(1)} %bitcast.162, f32[1,8,176,1408]{3,2,1,0:T(8,128)S(1)} %get-tuple-element.13, f32[8,176]{1,0:T(8,128)S(1)} %log_add_fusion, pred[176,1408]{1,0:T(8,128)(4,1)S(1)} %broadcast_compare_fusion, bf16[1408,1,2,128]{0,3,2,1:T(8,128)(2,1)S(1)} %bitcast.146, ...), kind=kOutput, calls=%fused_computation.10 | convolution fusion | flops 517423104 | bytes 12879872 | tf_op jit(solution)/shard_map/qgjd,kgd->gjqk/dot_general | solution.py:64
  94.0 0.0 copy-start.1
  94.0 0.9 fusion.13
  94.9 1.7 convolution_bitcast_fusion
  96.6 0.0 copy-done.1
  96.6 0.1 pad_maximum_fusion
  96.7 1.5 copy.38
  98.2 0.0 reduce-scatter.2.cloned.1.call-update
  98.2 0.1 copy.32
  98.3 0.9 broadcast_in_dim_reshape.7
  99.2 90.8 %reduce-scatter.2.cloned.1.call-done = f32[176,256]{1,0:T(8,128)} async-done(((f32[1408,256]{1,0:T(8,128)}), f32[176,256]{1,0:T(8,128)}) %reduce-scatter.2.cloned.1.call-update) | async-done | bytes 180240 | tf_op jit(solution)/shard_map/reduce_scatter | solution.py:74
  190.0 1.6 all_to_all.30
  191.6 7.0 %all-to-all-start.1 = ((f32[8,22,256]{2,1,0:T(8,128)}), f32[8,22,256]{2,1,0:T(8,128)S(1)}, u32[]{:S(2)}, u32[]{:S(2)}) async-start(f32[8,22,256]{2,1,0:T(8,128)} %all_to_all.30), calls=%async_computation.2 | async-start | bytes 393216 | tf_op jit(solution)/shard_map/all_to_all | solution.py:75
  198.6 3.3 %fusion.17 = bf16[176,1,8,128]{3,0,2,1:T(8,128)(2,1)S(1)} fusion(bf16[8,176,1408]{2,1,0:T(8,128)(2,1)} %copy-done.1, bf16[1408,1,2,128]{0,3,2,1:T(8,128)(2,1)S(1)} %bitcast.147), kind=kOutput, calls=%fused_computation.19 | convolution fusion | flops 507871232 | bytes 4685824 | tf_op jit(solution)/shard_map/gjqk,kgd->qgjd/dot_general | solution.py:67
  201.9 0.1 copy.35
  202.0 0.9 broadcast_in_dim_reshape.8
  202.9 2.2 %all-to-all-done.1 = f32[8,22,256]{2,1,0:T(8,128)S(1)} async-done(((f32[8,22,256]{2,1,0:T(8,128)}), f32[8,22,256]{2,1,0:T(8,128)S(1)}, u32[]{:S(2)}, u32[]{:S(2)}) %all-to-all-start.1) | async-done | bytes 180256 | tf_op jit(solution)/shard_map/all_to_all | solution.py:75
  205.1 0.1 copy.75
  205.2 0.7 fusion.29
  (10 shorter events, 0.1 us)
Async XLA Ops:
  7.2 18.5 %copy-start = (bf16[1,2,176,1024]{3,2,1,0:T(8,128)(2,1)S(1)}, bf16[1,2,176,1024]{3,2,1,0:T(8,128)(2,1)}, u32[]{:S(2)}) copy-start(bf16[1,2,176,1024]{3,2,1,0:T(8,128)(2,1)} %param.8) | copy-start | bytes 2162692
  7.2 78.0 %collective-permute-start.2 = (bf16[176,1024]{1,0:T(8,128)(2,1)}, bf16[176,1024]{1,0:T(8,128)(2,1)S(1)}, u32[]{:S(2)}, u32[]{:S(2)}) collective-permute-start(bf16[176,1024]{1,0:T(8,128)(2,1)} %bitcast.163), channel_id=1, source_target_pairs={{64,0},{128,64},{192,128},{256,192},{320,256},{384,320},{448,384},... | collective-permute-start | bytes 1081352 | tf_op jit(solution)/shard_map/ppermute | solution.py:13
  23.7 6.6 %collective-permute-start = (bf16[22,2048]{1,0:T(8,128)(2,1)S(1)}, bf16[22,2048]{1,0:T(8,128)(2,1)S(1)}, u32[]{:S(2)}, u32[]{:S(2)}) collective-permute-start(bf16[22,2048]{1,0:T(8,128)(2,1)S(1)} %reshape.167), channel_id=1, source_target_pairs={{448,0},{0,64},{64,128},{128,192},{192,256},{256,320},{320,384},{3... | collective-permute-start | bytes 270344 | tf_op jit(solution)/shard_map/ppermute | solution.py:13
  26.4 59.0 %collective-permute-start.1 = (bf16[176,1024]{1,0:T(8,128)(2,1)}, bf16[176,1024]{1,0:T(8,128)(2,1)S(1)}, u32[]{:S(2)}, u32[]{:S(2)}) collective-permute-start(bf16[176,1024]{1,0:T(8,128)(2,1)} %dynamic-slice_bitcast_fusion), channel_id=1, source_target_pairs={{448,0},{0,64},{64,128},{128,192},{192,256},{256,320},{320,384},{3... | collective-permute-start | bytes 1081352 | tf_op jit(solution)/shard_map/ppermute | solution.py:13
  31.0 12.3 %all-to-all-start = ((bf16[22,8,256]{2,0,1:T(8,128)(2,1)}), bf16[22,8,256]{2,0,1:T(8,128)(2,1)S(1)}, u32[]{:S(2)}, u32[]{:S(2)}) async-start(bf16[22,8,256]{2,0,1:T(8,128)(2,1)} %copy.27), calls=%async_computation | async-start | bytes 196608 | tf_op jit(solution)/shard_map/all_to_all | solution.py:41
  37.9 152.1 %reduce-scatter.2.cloned.1.call-start = ((), (), s32[]{:S(2)}) async-start(), calls=%async_computation.3 | async-start | bytes 1622016 | tf_op jit(solution)/shard_map/reduce_scatter | solution.py:74
  94.0 2.6 %copy-start.1 = (bf16[8,176,1408]{2,1,0:T(8,128)(2,1)}, bf16[8,176,1408]{2,1,0:T(8,128)(2,1)S(1)}, u32[]{:S(2)}) copy-start(bf16[8,176,1408]{2,1,0:T(8,128)(2,1)S(1)} %fusion.6) | copy-start | bytes 11894788
  191.6 13.5 %all-to-all-start.1 = ((f32[8,22,256]{2,1,0:T(8,128)}), f32[8,22,256]{2,1,0:T(8,128)S(1)}, u32[]{:S(2)}, u32[]{:S(2)}) async-start(f32[8,22,256]{2,1,0:T(8,128)} %all_to_all.30), calls=%async_computation.2 | async-start | bytes 393216 | tf_op jit(solution)/shard_map/all_to_all | solution.py:75
Sparse Core Ops, SparseCore 0:
  98.4 91.6 reduce-scatter.1
where the time goes:
time: 213 us
  waiting for transfers between devices  99.2 us (47%)
  blocking collectives  41.5 us (19%)
  starting transfers between devices  29.4 us (14%)
  between operations  16.2 us (8%)
  matrix products  12.3 us (6%)
  local copies, waits for them, and re-layouts  10.9 us (5%)
  other arithmetic  3.13 us (1%)
    reduce_scatter x1, waiting for transfers between devices, body(): lax.psum_scatter(grad_terms, 'ctx', scatter_dimension=0, tiled=True)  90.8 us
    all_gather x1, blocking collectives, body(): kv_full = lax.all_gather(kv_tok, 'ctx', axis=0, tiled=True)  41.5 us
    ppermute x3, starting transfers between devices, passed_along(): return lax.ppermute(block, axis, route)  15.4 us
    all_to_all x1, starting transfers between devices, body(): lax.all_to_all(kv_rows_in, 'tp', split_axis=1, concat_axis=0, tiled=True)  6.98 us
    all_to_all x1, starting transfers between devices, body(): lax.all_to_all(own_grads, 'tp', split_axis=0, concat_axis=1, tiled=True)  6.96 us
    all_to_all x1, waiting for transfers between devices, body(): lax.all_to_all(kv_rows_in, 'tp', split_axis=1, concat_axis=0, tiled=True)  5.15 us
  transfers between devices with their start and end apart: 6, of which 4 were waited for; matrix products, arithmetic and copies ran while one was open for 5% of the time, Pallas kernels for 0%

commit v1 on v0

--- a/solution.py
+++ b/solution.py
@@ -1,10 +1,22 @@
+import functools
 import jax
 import jax.numpy as jnp
 from jax import lax
 from jax.sharding import PartitionSpec as P
+from jax.lax import all_to_all, axis_size
 
 HEAD_DIM = 128
 NEG = -1e30
+
+
+def work_groups(frame, row_dim):
+    table = []
+    for _ in range(axis_size("ctx")):
+        table.append(frame)
+    return jnp.concatenate(all_to_all(jnp.stack(table, 0), "ctx", 0, 0), row_dim)
+
+
+_search_rails = functools.partial(work_groups, row_dim=0)
 
 
 def passed_along(block, axis, distance):
@@ -39,7 +51,7 @@
     queries, kv_rows_in = passed_along((q_send, kv_send), "section", 1)
     cotangent = passed_along(grad_out[0], "section", -1)
     kv_tok = lax.all_to_all(kv_rows_in, "tp", split_axis=1, concat_axis=0, tiled=True)
-    kv_full = lax.all_gather(kv_tok, "ctx", axis=0, tiled=True)
+    kv_full = _search_rails(kv_tok)
     kv_full = kv_full.reshape(seq_rows, kv_local, 2, head_size)
     key_heads = kv_full[:, :, 0, :]
     value_heads = kv_full[:, :, 1, :]

time: 213 us -> 192 us (0.901)
  blocking collectives: 41.5 us -> 0 us
  waiting for transfers between devices: 99.2 us -> 114 us
  local copies, waits for them, and re-layouts: 10.9 us -> 13.9 us
    all_gather x1 -> x0, blocking collectives: 41.5 us -> none  [body(): kv_full = lax.all_gather(kv_tok, 'ctx', axis=0, tiled=True)]
    ppermute x3, waiting for transfers between devices: 1.04 us -> 16.9 us  [passed_along(): return lax.ppermute(block, axis, route)]
    all_to_all x0 -> x1, starting transfers between devices: none -> 7.71 us  [work_groups(): all_to_all(jnp.stack(table, 0), 'ctx', 0, 0)]
    ppermute x3, starting transfers between devices: 15.4 us -> 10.2 us  [passed_along(): return lax.ppermute(block, axis, route)]
    all_to_all x1, waiting for transfers between devices: 5.15 us -> 1.92 us  [body(): lax.all_to_all(kv_rows_in, 'tp', split_axis=1, concat_axis=0, tiled=True)]
    all_to_all x0 -> x1, waiting for transfers between devices: none -> 3.15 us  [work_groups(): all_to_all(jnp.stack(table, 0), 'ctx', 0, 0)]
  transfers between devices with their start and end apart: 6 -> 7, of which waited for: 4 -> 6; matrix products, arithmetic and copies ran while one was open for 5% -> 5% of each run, Pallas kernels for 0% -> 0%
where the time goes in v1:
time: 192 us; the launch traced here: 191 us
  waiting for transfers between devices  114 us (59%)
  starting transfers between devices  31 us (16%)
  between operations  16.3 us (8%)
  local copies, waits for them, and re-layouts  13.9 us (7%)
  matrix products  13.1 us (7%)
  other arithmetic  3.21 us (2%)
    reduce_scatter x1, waiting for transfers between devices, body(): lax.psum_scatter(grad_terms, 'ctx', scatter_dimension=0, tiled=True)  89.8 us
    ppermute x3, waiting for transfers between devices, passed_along(): return lax.ppermute(block, axis, route)  16.9 us
    ppermute x3, starting transfers between devices, passed_along(): return lax.ppermute(block, axis, route)  10.2 us
    all_to_all x1, starting transfers between devices, work_groups(): all_to_all(jnp.stack(table, 0), 'ctx', 0, 0)  7.71 us
    all_to_all x1, starting transfers between devices, body(): lax.all_to_all(own_grads, 'tp', split_axis=0, concat_axis=1, tiled=True)  6.96 us
    all_to_all x1, starting transfers between devices, body(): lax.all_to_all(kv_rows_in, 'tp', split_axis=1, concat_axis=0, tiled=True)  6.12 us
  transfers between devices with their start and end apart: 7, of which 6 were waited for; matrix products, arithmetic and copies ran while one was open for 5% of the time, Pallas kernels for 0%

profile of v1, /device:TPU:1, one launch (start us, length us, event | category | flops | bytes accessed | tf_op | source)
XLA Modules:
  0.0 191.5 jit_solution(5629588958024853475)
XLA Ops:
  7.2 0.0 copy-start
  7.2 1.3 dynamic_slice.18
  10.4 1.5 dynamic-slice_reduce_fusion
  12.0 0.1 copy.25
  12.1 4.8 %collective-permute-start = (bf16[22,2048]{1,0:T(8,128)(2,1)S(1)}, bf16[22,2048]{1,0:T(8,128)(2,1)S(1)}, u32[]{:S(2)}, u32[]{:S(2)}) collective-permute-start(bf16[22,2048]{1,0:T(8,128)(2,1)S(1)} %reshape.167), channel_id=1, source_target_pairs={{448,0},{0,64},{64,128},{128,192},{192,256},{256,320},{320,384},{3... | collective-permute-start | bytes 270344 | tf_op jit(solution)/shard_map/ppermute | solution.py:25
  17.0 9.2 %collective-permute-done = bf16[22,2048]{1,0:T(8,128)(2,1)S(1)} collective-permute-done((bf16[22,2048]{1,0:T(8,128)(2,1)S(1)}, bf16[22,2048]{1,0:T(8,128)(2,1)S(1)}, u32[]{:S(2)}, u32[]{:S(2)}) %collective-permute-start) | collective-permute-done | bytes 90144 | tf_op jit(solution)/shard_map/ppermute | solution.py:25
  26.1 0.7 copy.26
  26.8 6.1 %all-to-all-start = ((bf16[22,8,256]{2,0,1:T(8,128)(2,1)}), bf16[22,8,256]{2,0,1:T(8,128)(2,1)S(1)}, u32[]{:S(2)}, u32[]{:S(2)}) async-start(bf16[22,8,256]{2,0,1:T(8,128)(2,1)} %copy.26), calls=%async_computation | async-start | bytes 196608 | tf_op jit(solution)/shard_map/all_to_all | solution.py:53
  32.9 3.4 %collective-permute-start.2 = (bf16[176,1024]{1,0:T(8,128)(2,1)}, bf16[176,1024]{1,0:T(8,128)(2,1)S(1)}, u32[]{:S(2)}, u32[]{:S(2)}) collective-permute-start(bf16[176,1024]{1,0:T(8,128)(2,1)} %bitcast.154), channel_id=1, source_target_pairs={{64,0},{128,64},{192,128},{256,192},{320,256},{384,320},{448,384},... | collective-permute-start | bytes 1081352 | tf_op jit(solution)/shard_map/ppermute | solution.py:25
  36.4 1.9 %all-to-all-done = bf16[22,8,256]{2,0,1:T(8,128)(2,1)S(1)} async-done(((bf16[22,8,256]{2,0,1:T(8,128)(2,1)}), bf16[22,8,256]{2,0,1:T(8,128)(2,1)S(1)}, u32[]{:S(2)}, u32[]{:S(2)}) %all-to-all-start) | async-done | bytes 90144 | tf_op jit(solution)/shard_map/all_to_all | solution.py:53
  38.3 0.9 stack.27
  39.3 7.7 %all-to-all-start.1 = ((bf16[8,176,256]{2,1,0:T(8,128)(2,1)}), bf16[8,176,256]{2,1,0:T(8,128)(2,1)S(1)}, u32[]{:S(2)}, u32[]{:S(2)}) async-start(bf16[8,176,256]{2,1,0:T(8,128)(2,1)} %stack.27), calls=%async_computation.1 | async-start | bytes 1441792 | tf_op jit(solution)/shard_map/all_to_all | solution.py:16
  47.0 0.0 reduce-scatter.2.cloned.1.call-start
  47.1 1.9 %collective-permute-start.1 = (bf16[176,1024]{1,0:T(8,128)(2,1)S(1)}, bf16[176,1024]{1,0:T(8,128)(2,1)S(1)}, u32[]{:S(2)}, u32[]{:S(2)}) collective-permute-start(bf16[176,1024]{1,0:T(8,128)(2,1)S(1)} %dynamic-slice_bitcast_fusion), channel_id=1, source_target_pairs={{448,0},{0,64},{64,128},{128,192},{192,256},{256,320},{320,384},{3... | collective-permute-start | bytes 1081352 | tf_op jit(solution)/shard_map/ppermute | solution.py:25
  49.0 0.7 broadcast_multiply_fusion
  49.7 0.1 iota_add_fusion
  49.7 0.1 add.59
  49.8 0.1 dynamic_slice.21
  49.9 0.2 broadcast_compare_fusion
  50.1 0.0 collective-permute-done.2
  50.1 0.1 convert_bitcast_fusion
  50.2 1.0 copy.45
  51.2 7.7 %collective-permute-done.1 = bf16[176,1024]{1,0:T(8,128)(2,1)S(1)} collective-permute-done((bf16[176,1024]{1,0:T(8,128)(2,1)S(1)}, bf16[176,1024]{1,0:T(8,128)(2,1)S(1)}, u32[]{:S(2)}, u32[]{:S(2)}) %collective-permute-start.1) | collective-permute-done | bytes 360480 | tf_op jit(solution)/shard_map/ppermute | solution.py:25
  58.9 0.1 copy.46
  59.0 3.1 %all-to-all-done.1 = bf16[8,176,256]{2,1,0:T(8,128)(2,1)S(1)} async-done(((bf16[8,176,256]{2,1,0:T(8,128)(2,1)}), bf16[8,176,256]{2,1,0:T(8,128)(2,1)S(1)}, u32[]{:S(2)}, u32[]{:S(2)}) %all-to-all-start.1) | async-done | bytes 720928 | tf_op jit(solution)/shard_map/all_to_all | solution.py:16
  62.1 0.2 reshape_reshape.3
  62.3 1.1 fusion.29
  63.3 0.0 copy-start.2
  63.4 1.9 fusion.31
  65.3 2.0 %select_reduce_fusion = f32[8,176]{1,0:T(8,128)S(1)} fusion(f32[1,8,176,1408]{3,2,1,0:T(8,128)S(1)} %get-tuple-element.15, f32[8,176]{1,0:T(8,128)S(1)} %get-tuple-element.14, pred[176,1408]{1,0:T(8,128)(4,1)S(1)} %broadcast_compare_fusion), kind=kLoop, calls=%fused_computation.5 | loop fusion | flops 5945984 | bytes 8188928 | tf_op jit(solution)/shard_map/reduce_sum | solution.py:68
  67.3 2.5 %fusion.18 = (f32[176,8]{0,1:T(8,128)S(1)}, bf16[176,1,8,128]{3,0,2,1:T(8,128)(2,1)}) fusion(f32[176,1,8,128]{3,2,0,1:T(8,128)S(1)} %bitcast.141, f32[1,8,176,1408]{3,2,1,0:T(8,128)S(1)} %get-tuple-element.15, f32[8,176]{1,0:T(8,128)S(1)} %log_add_fusion, pred[176,1408]{1,0:T(8,128)(4,1)S(1)} %broadcast_compare_fusion, ...), kind=kOutput, calls=%fused_computation.21 | convolution fusion | flops 513997440 | bytes 9630720 | tf_op jit(solution)/shard_map/gjqk,kgd->qgjd/dot_general | solution.py:72
  69.8 2.9 %fusion.6 = bf16[8,176,1408]{2,1,0:T(8,128)(2,1)S(1)} fusion(f32[8,176]{1,0:T(8,128)S(1)} %bitcast.153, f32[1,8,176,1408]{3,2,1,0:T(8,128)S(1)} %get-tuple-element.15, f32[8,176]{1,0:T(8,128)S(1)} %log_add_fusion, pred[176,1408]{1,0:T(8,128)(4,1)S(1)} %broadcast_compare_fusion, bf16[1408,1,1,128]{3,2,0,1:T(2,128)(2,1)S(1)} %get-tuple-element.10, ...), kind=kOutput, calls=%fused_computation.10 | convolution fusion | flops 517423104 | bytes 12874752 | tf_op jit(solution)/shard_map/qgjd,kgd->gjqk/dot_general | solution.py:76
  72.7 0.9 fusion.13
  73.6 1.7 convolution_bitcast_fusion
  75.3 0.2 pad_maximum_fusion
  75.4 1.5 copy.36
  77.0 0.0 reduce-scatter.2.cloned.1.call-update
  77.0 1.1 copy.30
  78.1 0.9 broadcast_in_dim_reshape.7
  79.0 89.8 %reduce-scatter.2.cloned.1.call-done = f32[176,256]{1,0:T(8,128)} async-done(((f32[1408,256]{1,0:T(8,128)}), f32[176,256]{1,0:T(8,128)}) %reduce-scatter.2.cloned.1.call-update) | async-done | bytes 180240 | tf_op jit(solution)/shard_map/reduce_scatter | solution.py:86
  168.7 1.6 all_to_all.31
  170.4 7.0 %all-to-all-start.2 = ((f32[8,22,256]{2,1,0:T(8,128)}), f32[8,22,256]{2,1,0:T(8,128)S(1)}, u32[]{:S(2)}, u32[]{:S(2)}) async-start(f32[8,22,256]{2,1,0:T(8,128)} %all_to_all.31), calls=%async_computation.3 | async-start | bytes 393216 | tf_op jit(solution)/shard_map/all_to_all | solution.py:87
  177.3 3.3 %fusion.17 = bf16[176,1,8,128]{3,0,2,1:T(8,128)(2,1)S(1)} fusion(bf16[8,176,1408]{2,1,0:T(8,128)(2,1)} %copy-done.1, bf16[1408,1,1,128]{3,2,0,1:T(2,128)(2,1)S(1)} %get-tuple-element.11), kind=kOutput, calls=%fused_computation.19 | convolution fusion | flops 507871232 | bytes 4685824 | tf_op jit(solution)/shard_map/gjqk,kgd->qgjd/dot_general | solution.py:79
  180.7 0.1 copy.33
  180.8 0.9 broadcast_in_dim_reshape.8
  181.6 2.2 %all-to-all-done.2 = f32[8,22,256]{2,1,0:T(8,128)S(1)} async-done(((f32[8,22,256]{2,1,0:T(8,128)}), f32[8,22,256]{2,1,0:T(8,128)S(1)}, u32[]{:S(2)}, u32[]{:S(2)}) %all-to-all-start.2) | async-done | bytes 180256 | tf_op jit(solution)/shard_map/all_to_all | solution.py:87
  183.9 0.1 copy.83
  183.9 0.7 fusion.30
  (15 shorter events, 0.2 us)
Async XLA Ops:
  7.2 39.8 %copy-start = (bf16[1,2,176,1024]{3,2,1,0:T(8,128)(2,1)S(1)}, bf16[1,2,176,1024]{3,2,1,0:T(8,128)(2,1)}, u32[]{:S(2)}) copy-start(bf16[1,2,176,1024]{3,2,1,0:T(8,128)(2,1)} %param.8) | copy-start | bytes 2162692
  12.1 14.0 %collective-permute-start = (bf16[22,2048]{1,0:T(8,128)(2,1)S(1)}, bf16[22,2048]{1,0:T(8,128)(2,1)S(1)}, u32[]{:S(2)}, u32[]{:S(2)}) collective-permute-start(bf16[22,2048]{1,0:T(8,128)(2,1)S(1)} %reshape.167), channel_id=1, source_target_pairs={{448,0},{0,64},{64,128},{128,192},{192,256},{256,320},{320,384},{3... | collective-permute-start | bytes 270344 | tf_op jit(solution)/shard_map/ppermute | solution.py:25
  26.8 11.5 %all-to-all-start = ((bf16[22,8,256]{2,0,1:T(8,128)(2,1)}), bf16[22,8,256]{2,0,1:T(8,128)(2,1)S(1)}, u32[]{:S(2)}, u32[]{:S(2)}) async-start(bf16[22,8,256]{2,0,1:T(8,128)(2,1)} %copy.26), calls=%async_computation | async-start | bytes 196608 | tf_op jit(solution)/shard_map/all_to_all | solution.py:53
  32.9 17.2 %collective-permute-start.2 = (bf16[176,1024]{1,0:T(8,128)(2,1)}, bf16[176,1024]{1,0:T(8,128)(2,1)S(1)}, u32[]{:S(2)}, u32[]{:S(2)}) collective-permute-start(bf16[176,1024]{1,0:T(8,128)(2,1)} %bitcast.154), channel_id=1, source_target_pairs={{64,0},{128,64},{192,128},{256,192},{320,256},{384,320},{448,384},... | collective-permute-start | bytes 1081352 | tf_op jit(solution)/shard_map/ppermute | solution.py:25
  39.3 22.9 %all-to-all-start.1 = ((bf16[8,176,256]{2,1,0:T(8,128)(2,1)}), bf16[8,176,256]{2,1,0:T(8,128)(2,1)S(1)}, u32[]{:S(2)}, u32[]{:S(2)}) async-start(bf16[8,176,256]{2,1,0:T(8,128)(2,1)} %stack.27), calls=%async_computation.1 | async-start | bytes 1441792 | tf_op jit(solution)/shard_map/all_to_all | solution.py:16
  47.0 121.8 %reduce-scatter.2.cloned.1.call-start = ((), (), s32[]{:S(2)}) async-start(), calls=%async_computation.4 | async-start | bytes 1622016 | tf_op jit(solution)/shard_map/reduce_scatter | solution.py:86
  47.1 11.8 %collective-permute-start.1 = (bf16[176,1024]{1,0:T(8,128)(2,1)S(1)}, bf16[176,1024]{1,0:T(8,128)(2,1)S(1)}, u32[]{:S(2)}, u32[]{:S(2)}) collective-permute-start(bf16[176,1024]{1,0:T(8,128)(2,1)S(1)} %dynamic-slice_bitcast_fusion), channel_id=1, source_target_pairs={{448,0},{0,64},{64,128},{128,192},{192,256},{256,320},{320,384},{3... | collective-permute-start | bytes 1081352 | tf_op jit(solution)/shard_map/ppermute | solution.py:25
  63.3 3.9 %copy-start.2 = (f32[22,8,8,128]{3,2,1,0:T(8,128)S(1)}, f32[22,8,8,128]{3,2,1,0:T(8,128)}, u32[]{:S(2)}) copy-start(f32[22,8,8,128]{3,2,1,0:T(8,128)} %copy.45) | copy-start | bytes 2162692
  72.7 2.6 %copy-start.1 = (bf16[8,176,1408]{2,1,0:T(8,128)(2,1)}, bf16[8,176,1408]{2,1,0:T(8,128)(2,1)S(1)}, u32[]{:S(2)}) copy-start(bf16[8,176,1408]{2,1,0:T(8,128)(2,1)S(1)} %fusion.6) | copy-start | bytes 11894788
  170.4 13.5 %all-to-all-start.2 = ((f32[8,22,256]{2,1,0:T(8,128)}), f32[8,22,256]{2,1,0:T(8,128)S(1)}, u32[]{:S(2)}, u32[]{:S(2)}) async-start(f32[8,22,256]{2,1,0:T(8,128)} %all_to_all.31), calls=%async_computation.3 | async-start | bytes 393216 | tf_op jit(solution)/shard_map/all_to_all | solution.py:87
Sparse Core Ops, SparseCore 0:
  77.1 91.5 reduce-scatter.1
